TPU v7x, 512 devices: a whole 4x8x8 slice. The times are simulated.
512 devices in a mesh: row: 32 (over z_hi, x, core), col: 16 (over z_lo, y).
Axes of the slice: x: 4, y: 8, z: 8 (z_hi: 4, z_lo: 2; z = z_hi * 2 + z_lo), core: 2. Of those that a mesh axis runs over, the one named last changes fastest.
Arguments:
- embeddings: float32 [16384, 768], P(('row', 'col')), may hold values from -0.21650635 to 0.21650635
- sharpness: float32 [16384], P(('row', 'col')), may hold values from 0.5 to 4
- soft_labels: float32 [16384, 256], P(('row', 'col')), may hold values from 0 to 1
- seed_mask: int32 [16384], P(('row', 'col')), may hold values 0 or 1
- tile_mask: int32 [512, 512], P('row'), may hold values from 0 to 1, as said below
Outputs:
- spread_labels: float32 [16384, 256], P(('row', 'col'))
Inputs may be any that keep to these rules, and one draw needn't show every extreme that they name: Every diagonal entry tile_mask[p, p] is 1.
All inputs are finite; a program needn't handle non-finite values. No bound on the sum of `seed_mask` on one device may be relied on, other than what follows from the above.
Results may differ from a plain program's by a relative error of at most 0.0003.
Values sent between devices are 32-bit elements; how exact they have to be, the bound alone decides.
No kernel may reach another device: no remote copies, remote signals or barrier semaphores. Data moves between devices by JAX's collectives and lax.ppermute only.
A program may use at most 64 MiB of HBM per device.

v0:
```python
import jax
import jax.numpy as jnp
from jax import lax
from jax.sharding import PartitionSpec as P

ITERS = 3


def kernel_tile(row_emb, row_squares, row_width, col_emb, col_width, col_mask):
    cross = jnp.dot(
        row_emb, col_emb.T, precision=lax.Precision.HIGHEST, preferred_element_type=jnp.float32
    )
    col_squares = jnp.sum(col_emb * col_emb, axis=1)
    distance = row_squares[:, None] + col_squares[None, :] - 2.0 * cross
    return jnp.exp(-(distance * row_width[:, None] * col_width[None, :])) * col_mask


def local(embeddings, sharpness, soft_labels, seed_mask, tile_mask):
    n_row = lax.axis_size("row")
    n_col = lax.axis_size("col")
    col_index = lax.axis_index("col")
    piece = embeddings.shape[0]
    seeded = seed_mask.astype(jnp.float32)[:, None] * soft_labels
    row_emb, row_width = (
        lax.all_gather(embeddings, "col", axis=0, tiled=True),
        lax.all_gather(sharpness, "col", axis=0, tiled=True),
    )
    row_squares = jnp.sum(row_emb * row_emb, axis=1)
    block_rows = row_emb.shape[0]
    col_rows = piece * n_row
    grouped = tile_mask.reshape(n_col, n_row, n_col)
    chosen = lax.dynamic_index_in_dim(grouped, col_index, axis=2, keepdims=False)
    col_mask = jnp.broadcast_to(chosen[:, None, :, None], (n_col, piece, n_row, piece))
    col_mask = col_mask.reshape(block_rows, col_rows).astype(jnp.float32)
    col_emb, col_width = (
        lax.all_gather(embeddings, "row", axis=0, tiled=True),
        lax.all_gather(sharpness, "row", axis=0, tiled=True),
    )
    labels = seeded
    for iteration in range(ITERS):
        col_labels = lax.all_gather(labels, "row", axis=0, tiled=True)
        weights = kernel_tile(row_emb, row_squares, row_width, col_emb, col_width, col_mask)
        partial_value = jnp.dot(
            weights, col_labels, precision=lax.Precision.HIGHEST, preferred_element_type=jnp.float32
        )
        degree = jnp.sum(weights, axis=1)
        total_part, total_degree = lax.psum((partial_value, degree), "col")
        own_part = lax.dynamic_slice_in_dim(total_part, col_index * piece, piece, 0)
        own_degree = lax.dynamic_slice_in_dim(total_degree, col_index * piece, piece, 0)
        labels = 0.9 * own_part / own_degree[:, None] + 0.1 * seeded
    return labels


def solution(mesh):
    return jax.shard_map(
        local,
        mesh=mesh,
        in_specs=(
            P(("row", "col"), None),
            P(("row", "col")),
            P(("row", "col"), None),
            P(("row", "col")),
            P("row", None),
        ),
        out_specs=P(("row", "col"), None),
        check_vma=False,
    )
```

profile of v0, /device:TPU:2, one launch (start us, length us, event | category | flops | bytes accessed | tf_op | source)
XLA Modules:
  0.0 762.3 jit_solution(18345925877665009551)
XLA Ops:
  6.5 0.7 all-gather.6.cloned.1.call-update
  7.3 0.0 all-gather.8.cloned.1.call-start
  7.3 0.7 all-gather.8.cloned.1.call-update
  8.0 0.0 all-gather.10.cloned.1.call-start
  8.1 0.7 convert_element_type.16
  8.7 1.4 broadcast_multiply_fusion
  10.2 0.0 all-gather.10.cloned.1.call-update
  10.2 0.0 all-reduce.6.cloned.1.call-start
  10.2 0.9 reshape.14
  11.1 0.3 convert_reduce_fusion
  11.4 4.4 broadcast_in_dim.2
  15.8 7.7 %convert_element_type.15 = f32[512,1024]{1,0:T(8,128)} reshape(f32[16,32,32,32]{3,2,1,0:T(8,128)} %broadcast_in_dim.2) | data formatting | bytes 4194304 | tf_op jit(solution)/shard_map/convert_element_type | solution.py:34
  23.5 1.3 dynamic-slice.1
  24.7 1.3 dynamic-slice
  27.4 0.0 copy-done.2
  27.4 0.2 dynamic-update-slice.1
  27.6 0.2 dynamic-update-slice
  27.8 35.9 %all-reduce = f32[512]{0:T(512)S(1)} all-reduce(f32[512]{0:T(512)S(1)} %dynamic-update-slice), channel_id=1, replica_groups=mesh['row'=32,'col'=16] {'col'}, use_global_device_ids=true, to_apply=%add | all-reduce | flops 512 | bytes 4096
  63.7 68.1 %all-reduce.1 = f32[1024]{0:T(1024)S(1)} all-reduce(f32[1024]{0:T(1024)S(1)} %dynamic-update-slice.1), channel_id=1, replica_groups=mesh['row'=32,'col'=16] {'row'}, use_global_device_ids=true, to_apply=%add.1 | all-reduce | flops 1024 | bytes 8192
  131.8 0.0 all-gather.6.cloned.1.call-done
  131.8 1.6 multiply_reduce_fusion.1
  133.4 16.2 %all-gather.8.cloned.1.call-done = f32[1024,768]{1,0:T(8,128)} async-done(((f32[32,768]{1,0:T(8,128)}), f32[1024,768]{1,0:T(8,128)}) %all-gather.8.cloned.1.call-update) | async-done | bytes 3145744 | tf_op jit(solution)/shard_map/all_gather | solution.py:36
  149.6 2.3 multiply_reduce_fusion
  151.9 0.5 copy-done
  152.4 7.7 %fusion = (f32[512]{0:T(512)S(1)}, f32[512,1024]{1,0:T(8,128)S(1)}) fusion(f32[512,1024]{1,0:T(8,128)} %convert_element_type.15, f32[1024]{0:T(1024)S(1)} %all-reduce.1, f32[512]{0:T(512)S(1)} %all-reduce, f32[512,768]{1,0:T(8,128)} %all-gather.6.cloned.1.call-done, f32[1024,768]{1,0:T(8,128)S(1)} %copy-done, f32[1024]{0:T(1024)S(1)} %multiply_reduce_fusion, ...), kind=kOutput, calls=%fused_computation.8 | convolution fusion | flops 4836032000 | bytes 8927232 | tf_op jit(solution)/shard_map/dot_general | solution.py:10
  160.1 47.2 %all-gather.10.cloned.1.call-done = f32[1024,256]{1,0:T(8,128)} async-done(((f32[32,256]{1,0:T(8,128)}), f32[1024,256]{1,0:T(8,128)}) %all-gather.10.cloned.1.call-update) | async-done | bytes 1048592 | tf_op jit(solution)/shard_map/all_gather | solution.py:41
  207.3 3.8 fusion.1
  211.1 0.0 all-reduce.6.cloned.1.call-update
  211.2 0.0 all-gather.12.cloned.1.call-start
  211.2 33.8 %psum.29 = f32[512]{0:T(512)S(1)} all-reduce(f32[512]{0:T(512)S(1)} %get-tuple-element.5), channel_id=1, replica_groups=mesh['row'=32,'col'=16] {'col'}, use_global_device_ids=true, to_apply=%region_4.5 | all-reduce | flops 512 | bytes 4096 | tf_op jit(solution)/shard_map/psum | solution.py:47
  245.0 0.1 dynamic_slice.20
  245.1 106.3 %all-reduce.6.cloned.1.call-done = f32[512,256]{1,0:T(8,128)} async-done(((f32[512,256]{1,0:T(8,128)}), f32[512,256]{1,0:T(8,128)}) %all-reduce.6.cloned.1.call-update) | async-done | bytes 524304 | tf_op jit(solution)/shard_map/psum | solution.py:47
  351.3 1.5 divide_add_fusion.2
  352.8 0.0 all-gather.12.cloned.1.call-update
  352.8 0.2 all-reduce.8.cloned.1.call-start
  353.0 55.5 %all-gather.12.cloned.1.call-done = f32[1024,256]{1,0:T(8,128)} async-done(((f32[32,256]{1,0:T(8,128)}), f32[1024,256]{1,0:T(8,128)}) %all-gather.12.cloned.1.call-update) | async-done | bytes 1048592 | tf_op jit(solution)/shard_map/all_gather | solution.py:41
  408.6 3.8 fusion.2
  412.4 0.0 all-reduce.8.cloned.1.call-update
  412.5 0.0 all-gather.14.cloned.1.call-start
  412.5 140.1 %all-reduce.8.cloned.1.call-done = f32[512,256]{1,0:T(8,128)} async-done(((f32[512,256]{1,0:T(8,128)}), f32[512,256]{1,0:T(8,128)}) %all-reduce.8.cloned.1.call-update) | async-done | bytes 524304 | tf_op jit(solution)/shard_map/psum | solution.py:47
  552.6 1.5 divide_add_fusion.1
  554.1 0.0 all-gather.14.cloned.1.call-update
  554.1 0.0 all-reduce.10.cloned.1.call-start
  554.1 55.9 %all-gather.14.cloned.1.call-done = f32[1024,256]{1,0:T(8,128)} async-done(((f32[32,256]{1,0:T(8,128)}), f32[1024,256]{1,0:T(8,128)}) %all-gather.14.cloned.1.call-update) | async-done | bytes 1048592 | tf_op jit(solution)/shard_map/all_gather | solution.py:41
  610.0 3.8 fusion.3
  613.9 0.0 all-reduce.10.cloned.1.call-update
  613.9 140.1 %all-reduce.10.cloned.1.call-done = f32[512,256]{1,0:T(8,128)} async-done(((f32[512,256]{1,0:T(8,128)}), f32[512,256]{1,0:T(8,128)}) %all-reduce.10.cloned.1.call-update) | async-done | bytes 524304 | tf_op jit(solution)/shard_map/psum | solution.py:47
  754.0 1.5 divide_add_fusion
  (7 shorter events, 0.0 us)
Async XLA Ops:
  6.5 125.3 %all-gather.6.cloned.1.call-start = ((), (), s32[]{:S(2)}) async-start(), calls=%async_computation | async-start | bytes 1671168 | tf_op jit(solution)/shard_map/all_gather | solution.py:25
  7.3 142.4 %all-gather.8.cloned.1.call-start = ((), (), s32[]{:S(2)}) async-start(), calls=%async_computation.1 | async-start | bytes 3244032 | tf_op jit(solution)/shard_map/all_gather | solution.py:36
  8.0 199.3 %all-gather.10.cloned.1.call-start = ((), (), s32[]{:S(2)}) async-start(), calls=%async_computation.2 | async-start | bytes 1081344 | tf_op jit(solution)/shard_map/all_gather | solution.py:41
  10.2 341.2 %all-reduce.6.cloned.1.call-start = ((), (), s32[]{:S(2)}) async-start(), calls=%async_computation.3 | async-start | bytes 1048576 | tf_op jit(solution)/shard_map/psum | solution.py:47
  15.8 11.6 %copy-start.2 = (f32[32]{0:T(128)S(1)}, f32[32]{0:T(128)}, u32[]{:S(2)}) copy-start(f32[32]{0:T(128)} %param.6) | copy-start | bytes 388
  149.6 2.8 copy-start
  207.3 144.0 %copy-start.1 = (f32[32,256]{1,0:T(8,128)S(1)}, f32[32,256]{1,0:T(8,128)}, u32[]{:S(2)}) copy-start(f32[32,256]{1,0:T(8,128)} %param.7) | copy-start | bytes 98308
  211.2 197.4 %all-gather.12.cloned.1.call-start = ((), (), s32[]{:S(2)}) async-start(), calls=%async_computation.4 | async-start | bytes 1081344 | tf_op jit(solution)/shard_map/all_gather | solution.py:41
  352.8 199.8 %all-reduce.8.cloned.1.call-start = ((), (), s32[]{:S(2)}) async-start(), calls=%async_computation.5 | async-start | bytes 1048576 | tf_op jit(solution)/shard_map/psum | solution.py:47
  412.5 197.5 %all-gather.14.cloned.1.call-start = ((), (), s32[]{:S(2)}) async-start(), calls=%async_computation.6 | async-start | bytes 1081344 | tf_op jit(solution)/shard_map/all_gather | solution.py:41
  554.1 199.9 %all-reduce.10.cloned.1.call-start = ((), (), s32[]{:S(2)}) async-start(), calls=%async_computation.7 | async-start | bytes 1048576 | tf_op jit(solution)/shard_map/psum | solution.py:47
Sparse Core Ops, SparseCore 0:
  9.4 77.4 all-gather.5
  90.0 59.5 all-gather.7
  152.8 54.5 all-gather.9
  211.3 140.0 all-reduce.5
  354.3 54.2 all-gather.11
  412.6 139.9 all-reduce.7
  555.7 54.2 all-gather.13
  614.0 139.9 all-reduce.9
where the time goes:
time: 763 us; the launch traced here: 762 us
  waiting for transfers between devices  563 us (74%)
  blocking collectives  138 us (18%)
  matrix products  19.2 us (3%)
  local copies, waits for them, and re-layouts  16.6 us (2%)
  between operations  14.8 us (2%)
  other arithmetic  10.6 us (1%)
    psum x3, waiting for transfers between devices, local(): total_part, total_degree = lax.psum((partial_value, degree), 'col')  387 us
    all_gather x3, waiting for transfers between devices, local(): col_labels = lax.all_gather(labels, 'row', axis=0, tiled=True)  159 us
    unnamed x2, blocking collectives  104 us
    psum x1, blocking collectives, local(): total_part, total_degree = lax.psum((partial_value, degree), 'col')  33.8 us
    all_gather x1, waiting for transfers between devices, local(): lax.all_gather(embeddings, 'row', axis=0, tiled=True)  16.2 us
  transfers between devices with their start and end apart: 8, of which 7 were waited for; matrix products, arithmetic and copies ran while one was open for 4% of the time, Pallas kernels for 0%

commit v1 on v0

--- a/solution.py
+++ b/solution.py
@@ -38,7 +38,9 @@
     )
     labels = seeded
     for iteration in range(ITERS):
-        col_labels = lax.all_gather(labels, "row", axis=0, tiled=True)
+        col_labels = jnp.concatenate(
+            lax.all_to_all(jnp.stack([labels] * lax.axis_size("row")), "row", 0, 0), axis=0
+        )
         weights = kernel_tile(row_emb, row_squares, row_width, col_emb, col_width, col_mask)
         partial_value = jnp.dot(
             weights, col_labels, precision=lax.Precision.HIGHEST, preferred_element_type=jnp.float32

time: 763 us -> 666 us (0.87)
  waiting for transfers between devices: 563 us -> 396 us
  blocking collectives: 138 us -> 200 us
  starting transfers between devices: 0.47 us -> 13.6 us
    all_gather x3 -> x0, waiting for transfers between devices: 159 us -> none  [local(): col_labels = lax.all_gather(labels, 'row', axis=0, tiled=True)]
    all_to_all x0 -> x2, blocking collectives: none -> 66.4 us  [local(): lax.all_to_all(jnp.stack([labels] * lax.axis_size('row')), 'row', 0, 0)]
    all_to_all x0 -> x1, starting transfers between devices: none -> 13.5 us  [local(): lax.all_to_all(jnp.stack([labels] * lax.axis_size('row')), 'row', 0, 0)]
  transfers between devices with their start and end apart: 8 -> 6, of which waited for: 7 -> 4; matrix products, arithmetic and copies ran while one was open for 4% -> 4% of each run, Pallas kernels for 0% -> 0%
where the time goes in v1:
time: 666 us; the launch traced here: 665 us
  waiting for transfers between devices  396 us (59%)
  blocking collectives  200 us (30%)
  local copies, waits for them, and re-layouts  17.3 us (3%)
  matrix products  15.6 us (2%)
  between operations  14.6 us (2%)
  starting transfers between devices  13.6 us (2%)
  other arithmetic  8.78 us (1%)
    psum x3, waiting for transfers between devices, local(): total_part, total_degree = lax.psum((partial_value, degree), 'col')  385 us
    unnamed x2, blocking collectives  99.2 us
    all_to_all x2, blocking collectives, local(): lax.all_to_all(jnp.stack([labels] * lax.axis_size('row')), 'row', 0, 0)  66.4 us
    psum x1, blocking collectives, local(): total_part, total_degree = lax.psum((partial_value, degree), 'col')  34.2 us
    all_to_all x1, starting transfers between devices, local(): lax.all_to_all(jnp.stack([labels] * lax.axis_size('row')), 'row', 0, 0)  13.5 us
  transfers between devices with their start and end apart: 6, of which 4 were waited for; matrix products, arithmetic and copies ran while one was open for 4% of the time, Pallas kernels for 0%

profile of v1, /device:TPU:2, one launch (start us, length us, event | category | flops | bytes accessed | tf_op | source)
XLA Modules:
  0.0 665.3 jit_solution(10481367444419149309)
XLA Ops:
  6.5 0.7 all-gather.3.cloned.1.call-update
  7.3 0.0 all-gather.5.cloned.1.call-start
  7.3 0.7 all-gather.5.cloned.1.call-update
  8.0 0.7 convert_element_type.16
  8.7 0.8 broadcast_multiply_fusion
  9.5 1.1 stack.6
  10.6 13.5 %all-to-all-start = ((f32[32,32,256]{2,1,0:T(8,128)}), f32[32,32,256]{2,1,0:T(8,128)S(1)}, u32[]{:S(2)}, u32[]{:S(2)}) async-start(f32[32,32,256]{2,1,0:T(8,128)} %stack.6), calls=%async_computation | async-start | bytes 2097152 | tf_op jit(solution)/shard_map/all_to_all | solution.py:42
  24.1 0.0 all-reduce.6.cloned.1.call-start
  24.1 0.0 copy-done.2
  24.2 0.1 reshape.29
  24.3 0.3 convert_reduce_fusion
  24.6 4.4 broadcast_in_dim.2
  28.9 7.8 %convert_element_type.15 = f32[512,1024]{1,0:T(8,128)} reshape(f32[16,32,32,32]{3,2,1,0:T(8,128)} %broadcast_in_dim.2) | data formatting | bytes 4194304 | tf_op jit(solution)/shard_map/convert_element_type | solution.py:34
  36.7 1.3 dynamic-slice.1
  37.9 1.3 dynamic-slice
  40.6 0.0 copy-done.3
  40.6 0.2 dynamic-update-slice.1
  40.9 0.2 dynamic-update-slice
  41.1 35.1 %all-reduce = f32[512]{0:T(512)S(1)} all-reduce(f32[512]{0:T(512)S(1)} %dynamic-update-slice), channel_id=1, replica_groups=mesh['row'=32,'col'=16] {'col'}, use_global_device_ids=true, to_apply=%add | all-reduce | flops 512 | bytes 4096
  76.2 64.1 %all-reduce.1 = f32[1024]{0:T(1024)S(1)} all-reduce(f32[1024]{0:T(1024)S(1)} %dynamic-update-slice.1), channel_id=1, replica_groups=mesh['row'=32,'col'=16] {'row'}, use_global_device_ids=true, to_apply=%add.1 | all-reduce | flops 1024 | bytes 8192
  140.3 0.0 all-gather.3.cloned.1.call-done
  140.3 1.6 multiply_reduce_fusion.1
  141.9 8.7 %all-gather.5.cloned.1.call-done = f32[1024,768]{1,0:T(8,128)} async-done(((f32[32,768]{1,0:T(8,128)}), f32[1024,768]{1,0:T(8,128)}) %all-gather.5.cloned.1.call-update) | async-done | bytes 3145744 | tf_op jit(solution)/shard_map/all_gather | solution.py:36
  150.6 2.3 multiply_reduce_fusion
  152.9 0.5 copy-done
  153.4 7.7 %fusion = (f32[512]{0:T(512)S(1)}, f32[512,1024]{1,0:T(8,128)S(1)}) fusion(f32[512,1024]{1,0:T(8,128)} %convert_element_type.15, f32[1024]{0:T(1024)S(1)} %all-reduce.1, f32[512]{0:T(512)S(1)} %all-reduce, f32[512,768]{1,0:T(8,128)} %all-gather.3.cloned.1.call-done, f32[1024,768]{1,0:T(8,128)S(1)} %copy-done, f32[1024]{0:T(1024)S(1)} %multiply_reduce_fusion, ...), kind=kOutput, calls=%fused_computation.8 | convolution fusion | flops 4836032000 | bytes 8927232 | tf_op jit(solution)/shard_map/dot_general | solution.py:10
  161.1 0.0 all-to-all-done
  161.1 0.0 copy-start.1
  161.2 2.6 fusion.1
  163.8 0.0 all-reduce.6.cloned.1.call-update
  163.8 0.0 all-reduce.8.cloned.1.call-start
  163.9 34.2 %psum.29 = f32[512]{0:T(512)S(1)} all-reduce(f32[512]{0:T(512)S(1)} %get-tuple-element.5), channel_id=1, replica_groups=mesh['row'=32,'col'=16] {'col'}, use_global_device_ids=true, to_apply=%region_4.5 | all-reduce | flops 512 | bytes 4096 | tf_op jit(solution)/shard_map/psum | solution.py:49
  198.1 0.1 dynamic_slice.20
  198.2 105.2 %all-reduce.6.cloned.1.call-done = f32[512,256]{1,0:T(8,128)} async-done(((f32[512,256]{1,0:T(8,128)}), f32[512,256]{1,0:T(8,128)}) %all-reduce.6.cloned.1.call-update) | async-done | bytes 524304 | tf_op jit(solution)/shard_map/psum | solution.py:49
  303.3 0.8 divide_add_fusion.2
  304.2 0.1 stack.7
  304.3 33.2 %all_to_all.15 = f32[32,32,256]{2,1,0:T(8,128)S(1)} all-to-all(f32[32,32,256]{2,1,0:T(8,128)S(1)} %stack.7), channel_id=1, replica_groups=mesh['row'=32,'col'=16] {'row'}, dimensions={0} | all-to-all | bytes 2097152 | tf_op jit(solution)/shard_map/all_to_all | solution.py:42
  337.5 2.6 fusion.2
  340.1 0.0 all-reduce.8.cloned.1.call-update
  340.1 0.0 all-reduce.10.cloned.1.call-start
  340.2 140.1 %all-reduce.8.cloned.1.call-done = f32[512,256]{1,0:T(8,128)} async-done(((f32[512,256]{1,0:T(8,128)}), f32[512,256]{1,0:T(8,128)}) %all-reduce.8.cloned.1.call-update) | async-done | bytes 524304 | tf_op jit(solution)/shard_map/psum | solution.py:49
  480.3 0.8 divide_add_fusion.1
  481.2 0.1 stack.8
  481.3 33.2 %all_to_all.16 = f32[32,32,256]{2,1,0:T(8,128)S(1)} all-to-all(f32[32,32,256]{2,1,0:T(8,128)S(1)} %stack.8), channel_id=1, replica_groups=mesh['row'=32,'col'=16] {'row'}, dimensions={0} | all-to-all | bytes 2097152 | tf_op jit(solution)/shard_map/all_to_all | solution.py:42
  514.5 2.6 fusion.3
  517.1 0.0 all-reduce.10.cloned.1.call-update
  517.1 140.2 %all-reduce.10.cloned.1.call-done = f32[512,256]{1,0:T(8,128)} async-done(((f32[512,256]{1,0:T(8,128)}), f32[512,256]{1,0:T(8,128)}) %all-reduce.10.cloned.1.call-update) | async-done | bytes 524304 | tf_op jit(solution)/shard_map/psum | solution.py:49
  657.3 1.5 divide_add_fusion
  (7 shorter events, 0.0 us)
Async XLA Ops:
  6.5 17.6 %copy-start.2 = (s32[16,512]{1,0:T(8,128)S(1)}, s32[16,512]{1,0:T(8,128)}, u32[]{:S(2)}) copy-start(s32[16,512]{1,0:T(8,128)} %param.9) | copy-start | bytes 98308
  6.5 133.7 %all-gather.3.cloned.1.call-start = ((), (), s32[]{:S(2)}) async-start(), calls=%async_computation.3 | async-start | bytes 1671168 | tf_op jit(solution)/shard_map/all_gather | solution.py:25
  7.3 143.3 %all-gather.5.cloned.1.call-start = ((), (), s32[]{:S(2)}) async-start(), calls=%async_computation.4 | async-start | bytes 3244032 | tf_op jit(solution)/shard_map/all_gather | solution.py:36
  10.6 150.5 %all-to-all-start = ((f32[32,32,256]{2,1,0:T(8,128)}), f32[32,32,256]{2,1,0:T(8,128)S(1)}, u32[]{:S(2)}, u32[]{:S(2)}) async-start(f32[32,32,256]{2,1,0:T(8,128)} %stack.6), calls=%async_computation | async-start | bytes 2097152 | tf_op jit(solution)/shard_map/all_to_all | solution.py:42
  24.1 279.2 %all-reduce.6.cloned.1.call-start = ((), (), s32[]{:S(2)}) async-start(), calls=%async_computation.5 | async-start | bytes 1048576 | tf_op jit(solution)/shard_map/psum | solution.py:49
  28.9 11.7 %copy-start.3 = (f32[32]{0:T(128)S(1)}, f32[32]{0:T(128)}, u32[]{:S(2)}) copy-start(f32[32]{0:T(128)} %param.6) | copy-start | bytes 388
  150.6 2.8 copy-start
  161.1 142.2 %copy-start.1 = (f32[32,256]{1,0:T(8,128)S(1)}, f32[32,256]{1,0:T(8,128)}, u32[]{:S(2)}) copy-start(f32[32,256]{1,0:T(8,128)} %param.7) | copy-start | bytes 98308
  163.8 316.5 %all-reduce.8.cloned.1.call-start = ((), (), s32[]{:S(2)}) async-start(), calls=%async_computation.6 | async-start | bytes 1048576 | tf_op jit(solution)/shard_map/psum | solution.py:49
  340.1 317.2 %all-reduce.10.cloned.1.call-start = ((), (), s32[]{:S(2)}) async-start(), calls=%async_computation.7 | async-start | bytes 1048576 | tf_op jit(solution)/shard_map/psum | solution.py:49
Sparse Core Ops, SparseCore 0:
  9.4 78.8 all-gather.2
  91.4 59.1 all-gather.4
  163.9 139.3 all-reduce.5
  340.3 140.0 all-reduce.7
  517.3 139.9 all-reduce.9
